TPU v7x, 256 devices: a whole 4x4x8 slice. The times are simulated.
256 devices in a mesh: dp: 64 (over y_hi, z, x), mp: 4 (over y_lo, core).
Axes of the slice: x: 4, y: 4 (y_hi: 2, y_lo: 2; y = y_hi * 2 + y_lo), z: 8, core: 2. Of those that a mesh axis runs over, the one named last changes fastest.
Arguments:
- image_feats: bfloat16 [65536, 1152], P('dp'), may hold values from -16 to 16
- text_feats: bfloat16 [65536, 1152], P('dp'), may hold values from -16 to 16
- image_head: bfloat16 [1152, 1152], P(None, 'mp')
- text_head: bfloat16 [1152, 1152], P(None, 'mp')
- hard_tiles: int32 [512, 16], P('dp'), may hold values from 0 to 511, as said below
- logit_scale: float32 [1], replicated, may hold values from 6 to 16
- logit_bias: float32 [1], replicated, may hold values from -4 to -1
Outputs:
- head_grad_img: float32 [1152, 1152], P('dp', 'mp')
- head_grad_txt: float32 [1152, 1152], P('dp', 'mp')
Inputs may be any that keep to these rules, and one draw needn't show every extreme that they name: `hard_tiles`: row tile g lies in block i = g // 8; with o running over -2 .. -1, 1 .. 2 in order as o_0 .. o_(3), entries 4 * k to 4 * k + 3 of row g are 4 different tiles of block (i + o_k) mod 64, and block j holds tiles 8 * j to 8 * j + 7.
All inputs are finite; a program needn't handle non-finite values.
Results may differ from a plain program's by a relative error of at most 0.0015.
Values may be sent and summed in bfloat16 or wider, within the bound.
No kernel may reach another device: no remote copies, remote signals or barrier semaphores. Data moves between devices by JAX's collectives and lax.ppermute only.
A program may use at most 128 MiB of HBM per device.

v0:
```python
import jax
import jax.numpy as jnp
from jax import lax
from jax.sharding import PartitionSpec as P

EPSILON = 1e-06


def shifted(value, axis, steps):
    count = lax.axis_size(axis)
    pairs = [(source, (source + steps) % count) for source in range(count)]
    return lax.ppermute(value, axis, pairs)


def shards(image_feats, text_feats, image_head, text_head, hard_tiles, logit_scale, logit_bias):
    row_count = image_feats.shape[0]
    width_part = image_head.shape[1]
    per_block = row_count // 128
    model_count = lax.axis_size("mp")
    model_index = lax.axis_index("mp")
    tiles_share = per_block // model_count
    span_blocks = min(2, (lax.axis_size("dp") - 1) // 2)
    pick_count = hard_tiles.shape[1] // (2 * span_blocks)
    temp_scale = logit_scale[0]
    shift_bias = logit_bias[0]
    image_proj = jnp.dot(image_feats, image_head, preferred_element_type=jnp.float32)
    text_proj = jnp.dot(text_feats, text_head, preferred_element_type=jnp.float32)
    norm_img, norm_txt = lax.psum(
        (jnp.sum(image_proj * image_proj, axis=1), jnp.sum(text_proj * text_proj, axis=1)), "mp"
    )
    inverse_img = lax.rsqrt(norm_img + EPSILON)
    inverse_txt = lax.rsqrt(norm_txt + EPSILON)
    image_unit = (image_proj * inverse_img[:, None]).astype(jnp.bfloat16)
    text_unit = (text_proj * inverse_txt[:, None]).astype(jnp.bfloat16)
    image_tiles = image_unit.reshape(per_block, 128, width_part)
    local_ids = hard_tiles % per_block
    image_mine = lax.all_to_all(image_unit, "mp", split_axis=0, concat_axis=1, tiled=True)
    mine_tiles = image_mine.reshape(tiles_share, 128, image_mine.shape[1])
    text_full = lax.all_gather(text_unit, "mp", axis=1, tiled=True)
    partial_value = jnp.dot(image_unit, text_unit.T, preferred_element_type=jnp.float32)
    scores = lax.psum(partial_value, "mp")
    diagonal_mask = jnp.eye(row_count, dtype=jnp.float32)
    weight = (
        temp_scale * (jax.nn.sigmoid(temp_scale * scores + shift_bias) - diagonal_mask)
    ).astype(jnp.bfloat16)
    grad_img = jnp.dot(weight, text_unit, preferred_element_type=jnp.float32)
    grad_txt = jnp.einsum("pq,pe->qe", weight, image_unit, preferred_element_type=jnp.float32)
    current = shifted(text_full, "dp", -span_blocks)
    carried = jnp.zeros_like(text_proj)
    for step_index in range(2 * span_blocks + 1):
        if step_index > 0:
            current = shifted(current, "dp", 1)
            carried = shifted(carried, "dp", 1)
        offset = span_blocks - step_index
        if offset != 0:
            slot_index = offset + span_blocks if offset < 0 else offset + span_blocks - 1
            picked = local_ids[:, pick_count * slot_index : pick_count * slot_index + pick_count]
            picked_mine = lax.dynamic_slice_in_dim(
                picked, model_index * tiles_share, tiles_share, 0
            )
            wide_tiles = current.reshape(per_block, 128, current.shape[1])
            chosen_wide = jnp.take(wide_tiles, picked_mine, axis=0)
            pair_part = jnp.einsum(
                "rpe,rkqe->rkpq", mine_tiles, chosen_wide, preferred_element_type=jnp.float32
            )
            weight_part = (temp_scale * jax.nn.sigmoid(temp_scale * pair_part + shift_bias)).astype(
                jnp.bfloat16
            )
            pair_weight = lax.all_gather(weight_part, "mp", axis=0, tiled=True)
            text_local = lax.dynamic_slice_in_dim(current, model_index * width_part, width_part, 1)
            chosen = jnp.take(text_local.reshape(per_block, 128, width_part), picked, axis=0)
            into_img = jnp.einsum(
                "rkpq,rkqe->rpe", pair_weight, chosen, preferred_element_type=jnp.float32
            )
            into_sel = jnp.einsum(
                "rkpq,rpe->rkqe", pair_weight, image_tiles, preferred_element_type=jnp.float32
            )
            onehot = (
                picked[:, :, None] == jnp.arange(per_block, dtype=jnp.int32)[None, None, :]
            ).astype(jnp.float32)
            into_txt = jnp.einsum(
                "rkt,rkqe->tqe", onehot, into_sel, precision=lax.Precision.HIGHEST
            )
            into_img, into_txt = (
                into_img.reshape(row_count, width_part),
                into_txt.reshape(row_count, width_part),
            )
            grad_img = grad_img + into_img
            carried = carried + into_txt
    grad_txt = grad_txt + shifted(carried, "dp", -span_blocks)
    dots_img, dots_txt = lax.psum(
        (jnp.sum(image_proj * grad_img, axis=1), jnp.sum(text_proj * grad_txt, axis=1)), "mp"
    )
    cube_img = dots_img * inverse_img * inverse_img * inverse_img
    cube_txt = dots_txt * inverse_txt * inverse_txt * inverse_txt
    dproj_img = (inverse_img[:, None] * grad_img - cube_img[:, None] * image_proj).astype(
        jnp.bfloat16
    )
    dproj_txt = (inverse_txt[:, None] * grad_txt - cube_txt[:, None] * text_proj).astype(
        jnp.bfloat16
    )
    local_img = jnp.einsum("nd,ne->de", image_feats, dproj_img, preferred_element_type=jnp.float32)
    local_txt = jnp.einsum("nd,ne->de", text_feats, dproj_txt, preferred_element_type=jnp.float32)
    head_grad_img, head_grad_txt = (
        lax.psum_scatter(local_img, "dp", scatter_dimension=0, tiled=True),
        lax.psum_scatter(local_txt, "dp", scatter_dimension=0, tiled=True),
    )
    return (head_grad_img, head_grad_txt)


def solution(mesh):
    placed = (P("dp", None), P("dp", None), P(None, "mp"), P(None, "mp"), P("dp", None), P(), P())
    return jax.shard_map(
        shards,
        mesh=mesh,
        in_specs=placed,
        out_specs=(P("dp", "mp"), P("dp", "mp")),
        check_vma=False,
    )
```

profile of v0, /device:TPU:24, one launch (start us, length us, event | category | flops | bytes accessed | tf_op | source)
XLA Modules:
  0.0 1375.7 jit_solution(13354665672646321138)
XLA Ops:
  8.8 3.2 multiply_reduce_fusion.3
  13.0 6.3 all-reduce.4
  20.3 36.2 %all-gather.6.cloned.1.call-done = bf16[1024,1152]{0,1:T(8,128)(2,1)} async-done(((bf16[1024,288]{0,1:T(8,128)(2,1)}), bf16[1024,1152]{0,1:T(8,128)(2,1)}) %all-gather.6.cloned.1.call-update) | async-done | bytes 2359312 | tf_op jit(solution)/shard_map/all_gather | solution.py:39
  56.5 6.3 collective-permute-start
  62.8 51.6 %collective-permute-done = bf16[1024,1152]{0,1:T(8,128)(2,1)} collective-permute-done((bf16[1024,1152]{0,1:T(8,128)(2,1)}, bf16[1024,1152]{0,1:T(8,128)(2,1)}, u32[]{:S(2)}, u32[]{:S(2)}) %collective-permute-start) | collective-permute-done | bytes 2359328 | tf_op jit(solution)/shard_map/ppermute | solution.py:12
  118.1 5.0 all-to-all-start
  128.9 51.7 %all-to-all-done = bf16[4,256,288]{1,2,0:T(8,128)(2,1)} async-done(((bf16[4,256,288]{1,2,0:T(8,128)(2,1)}), bf16[4,256,288]{1,2,0:T(8,128)(2,1)}, u32[]{:S(2)}, u32[]{:S(2)}) %all-to-all-start) | async-done | bytes 589856 | tf_op jit(solution)/shard_map/all_to_all | solution.py:37
  180.5 2.5 reshape.81
  183.1 2.9 copy.125
  186.0 4.3 copy.141
  190.3 4.0 gather_fusion
  194.3 3.3 fusion.160
  197.7 1.8 copy.93
  203.4 4.3 copy.144
  207.7 4.0 gather_fusion.2
  211.7 3.3 fusion.148
  215.0 1.8 copy.98
  216.9 4.5 fusion.197
  221.5 40.0 %collective-permute-done.2 = bf16[1024,1152]{0,1:T(8,128)(2,1)} collective-permute-done((bf16[1024,1152]{0,1:T(8,128)(2,1)}, bf16[1024,1152]{0,1:T(8,128)(2,1)}, u32[]{:S(2)}, u32[]{:S(2)}) %collective-permute-start.2) | collective-permute-done | bytes 2359328 | tf_op jit(solution)/shard_map/ppermute | solution.py:12
  282.0 2.2 fusion.168
  284.2 6.1 fusion.6
  293.4 28.5 %collective-permute-done.3 = bf16[1024,1152]{0,1:T(8,128)(2,1)} collective-permute-done((bf16[1024,1152]{0,1:T(8,128)(2,1)}, bf16[1024,1152]{0,1:T(8,128)(2,1)}, u32[]{:S(2)}, u32[]{:S(2)}) %collective-permute-start.3) | collective-permute-done | bytes 2359328 | tf_op jit(solution)/shard_map/ppermute | solution.py:12
  322.1 80.4 %all-gather.10.cloned.1.call-done = bf16[8,4,128,128]{3,2,1,0:T(8,128)(2,1)} async-done(((bf16[2,4,128,128]{3,2,1,0:T(8,128)(2,1)}), bf16[8,4,128,128]{3,2,1,0:T(8,128)(2,1)}) %all-gather.10.cloned.1.call-update) | async-done | bytes 1048592 | tf_op jit(solution)/shard_map/all_gather | solution.py:69
  402.5 2.2 fusion.170
  404.7 6.1 fusion.4
  410.8 2.9 bitcast_add_fusion.2
  413.7 4.3 copy.147
  418.0 4.1 gather_fusion.4
  422.0 3.3 fusion.136
  425.4 1.8 copy.103
  427.2 85.8 %all-reduce.8.cloned.1.call-done = f32[1024,1024]{1,0:T(8,128)} async-done(((f32[1024,1024]{1,0:T(8,128)}), f32[1024,1024]{1,0:T(8,128)}) %all-reduce.8.cloned.1.call-update) | async-done | bytes 4194320 | tf_op jit(solution)/shard_map/psum | solution.py:41
  513.0 4.7 multiply_convert_fusion
  517.7 2.0 copy_bitcast_fusion.4
  519.7 3.4 gather_fusion.1
  523.1 3.8 fusion.32
  527.0 1.9 collective-permute-start.7
  528.8 4.4 copy.150
  533.2 4.1 gather_fusion.6
  537.3 3.3 fusion.124
  540.6 1.8 copy.108
  542.5 2.0 copy_bitcast_fusion.3
  544.5 3.3 gather_fusion.3
  547.8 16.5 %all-gather.12.cloned.1.call-done = bf16[8,4,128,128]{3,2,1,0:T(8,128)(2,1)} async-done(((bf16[2,4,128,128]{3,2,1,0:T(8,128)(2,1)}), bf16[8,4,128,128]{3,2,1,0:T(8,128)(2,1)}) %all-gather.12.cloned.1.call-update) | async-done | bytes 1048592 | tf_op jit(solution)/shard_map/all_gather | solution.py:69
  564.3 2.2 fusion.172
  566.5 6.1 fusion.2
  572.6 2.8 bitcast_add_fusion.1
  575.7 1.9 fusion.35
  577.5 2.0 copy_bitcast_fusion.2
  579.6 3.3 gather_fusion.5
  582.9 2.2 fusion.174
  585.0 6.1 fusion
  591.2 36.0 %collective-permute-done.8 = f32[1024,288]{0,1:T(8,128)} collective-permute-done((f32[1024,288]{0,1:T(8,128)}, f32[1024,288]{0,1:T(8,128)}, u32[]{:S(2)}, u32[]{:S(2)}) %collective-permute-start.8) | collective-permute-done | bytes 1179680 | tf_op jit(solution)/shard_map/ppermute | solution.py:12
  627.2 2.6 bitcast_add_fusion
  630.1 1.9 fusion.38
  632.0 2.0 copy_bitcast_fusion.1
  634.0 3.3 gather_fusion.7
  637.3 3.0 fusion.41
  640.7 3.8 multiply_reduce_fusion.1
  644.5 14.9 %collective-permute-done.9 = f32[1024,288]{0,1:T(8,128)} collective-permute-done((f32[1024,288]{0,1:T(8,128)}, f32[1024,288]{0,1:T(8,128)}, u32[]{:S(2)}, u32[]{:S(2)}) %collective-permute-start.9) | collective-permute-done | bytes 1179680 | tf_op jit(solution)/shard_map/ppermute | solution.py:12
  659.5 3.1 multiply_reduce_fusion
  662.6 6.7 all-reduce.3
  670.0 3.8 convolution_bitcast_fusion.1
  673.9 3.5 convolution_bitcast_fusion
  679.2 685.8 %all-reduce.10.cloned.1.call-done = (f32[1152,288]{0,1:T(8,128)}, f32[1152,288]{0,1:T(8,128)}) async-done(((f32[1152,288]{0,1:T(8,128)}, f32[1152,288]{0,1:T(8,128)}), (f32[1152,288]{0,1:T(8,128)}, f32[1152,288]{0,1:T(8,128)})) %all-reduce.10.cloned.1.call-update) | async-done | bytes 2654224
  (139 shorter events, 46.1 us)
Async XLA Ops:
  7.2 1.7 copy-start
  7.2 49.3 %all-gather.6.cloned.1.call-start = ((), (), s32[]{:S(2)}) async-start(), calls=%async_computation.2 | async-start | bytes 2949120 | tf_op jit(solution)/shard_map/all_gather | solution.py:39
  8.8 3.2 copy-start.9
  8.8 3.2 copy-start.32
  19.3 43.5 %copy-start.16 = (f32[1024]{0:T(1024)}, f32[1024]{0:T(1024)S(1)}, u32[]{:S(2)}) copy-start(f32[1024]{0:T(1024)S(1)} %get-tuple-element.17) | copy-start | bytes 12292
  19.3 98.8 %copy-start.15 = (f32[1024]{0:T(1024)}, f32[1024]{0:T(1024)S(1)}, u32[]{:S(2)}) copy-start(f32[1024]{0:T(1024)S(1)} %get-tuple-element.16) | copy-start | bytes 12292
  20.3 104.1 %copy-start.24 = (s32[8,16]{1,0:T(8,128)S(1)}, s32[8,16]{1,0:T(8,128)}, u32[]{:S(2)}) copy-start(s32[8,16]{1,0:T(8,128)} %param.15) | copy-start | bytes 1540
  56.5 57.9 %collective-permute-start = (bf16[1024,1152]{0,1:T(8,128)(2,1)}, bf16[1024,1152]{0,1:T(8,128)(2,1)}, u32[]{:S(2)}, u32[]{:S(2)}) collective-permute-start(bf16[1024,1152]{0,1:T(8,128)(2,1)} %all-gather.6.cloned.1.call-done), channel_id=1, source_target_pairs={{0,248},{4,252},{8,0},{12,4},{16,8},{20,12},{24,16},{28,20},{32,24... | collective-permute-start | bytes 7077896 | tf_op jit(solution)/shard_map/ppermute | solution.py:12
  114.4 87.7 %collective-permute-start.1 = (bf16[1024,1152]{0,1:T(8,128)(2,1)}, bf16[1024,1152]{0,1:T(8,128)(2,1)}, u32[]{:S(2)}, u32[]{:S(2)}) collective-permute-start(bf16[1024,1152]{0,1:T(8,128)(2,1)} %collective-permute-done), channel_id=1, source_target_pairs={{0,4},{4,8},{8,12},{12,16},{16,20},{20,24},{24,28},{28,32},{32,36}... | collective-permute-start | bytes 7077896 | tf_op jit(solution)/shard_map/ppermute | solution.py:12
  116.4 0.8 copy-start.3
  118.1 62.4 %all-to-all-start = ((bf16[4,256,288]{1,2,0:T(8,128)(2,1)}), bf16[4,256,288]{1,2,0:T(8,128)(2,1)}, u32[]{:S(2)}, u32[]{:S(2)}) async-start(bf16[4,256,288]{1,2,0:T(8,128)(2,1)} %bitcast.192), calls=%async_computation | async-start | bytes 1179648 | tf_op jit(solution)/shard_map/all_to_all | solution.py:37
  123.1 158.9 %all-gather.8.cloned.1.call-start = ((), (), s32[]{:S(2)}) async-start(), calls=%async_computation.3 | async-start | bytes 1310720 | tf_op jit(solution)/shard_map/all_gather | solution.py:69
  125.1 0.6 copy-start.14
  199.5 203.1 %all-gather.10.cloned.1.call-start = ((), (), s32[]{:S(2)}) async-start(), calls=%async_computation.4 | async-start | bytes 1310720 | tf_op jit(solution)/shard_map/all_gather | solution.py:69
  202.1 59.4 %collective-permute-start.2 = (bf16[1024,1152]{0,1:T(8,128)(2,1)}, bf16[1024,1152]{0,1:T(8,128)(2,1)}, u32[]{:S(2)}, u32[]{:S(2)}) collective-permute-start(bf16[1024,1152]{0,1:T(8,128)(2,1)} %collective-permute-done.1), channel_id=1, source_target_pairs={{0,4},{4,8},{8,12},{12,16},{16,20},{20,24},{24,28},{28,32},{32,36}... | collective-permute-start | bytes 7077896 | tf_op jit(solution)/shard_map/ppermute | solution.py:12
  216.9 296.2 %all-reduce.8.cloned.1.call-start = ((), (), s32[]{:S(2)}) async-start(), calls=%async_computation.1 | async-start | bytes 8388608 | tf_op jit(solution)/shard_map/psum | solution.py:41
  221.5 342.8 %all-gather.12.cloned.1.call-start = ((), (), s32[]{:S(2)}) async-start(), calls=%async_computation.5 | async-start | bytes 1310720 | tf_op jit(solution)/shard_map/all_gather | solution.py:69
  261.5 60.4 %collective-permute-start.3 = (bf16[1024,1152]{0,1:T(8,128)(2,1)}, bf16[1024,1152]{0,1:T(8,128)(2,1)}, u32[]{:S(2)}, u32[]{:S(2)}) collective-permute-start(bf16[1024,1152]{0,1:T(8,128)(2,1)} %collective-permute-done.2), channel_id=1, source_target_pairs={{0,4},{4,8},{8,12},{12,16},{16,20},{20,24},{24,28},{28,32},{32,36}... | collective-permute-start | bytes 7077896 | tf_op jit(solution)/shard_map/ppermute | solution.py:12
  274.7 4.9 copy-start.30
  282.0 2.2 copy-start.23
  290.3 1.3 copy-start.26
  290.3 1.9 copy-start.25
  291.6 119.2 %collective-permute-start.5 = (f32[1024,288]{0,1:T(8,128)}, f32[1024,288]{0,1:T(8,128)}, u32[]{:S(2)}, u32[]{:S(2)}) collective-permute-start(f32[1024,288]{0,1:T(8,128)} %bitcast.159), channel_id=1, source_target_pairs={{0,4},{4,8},{8,12},{12,16},{16,20},{20,24},{24,28},{28,32},{32,36}... | collective-permute-start | bytes 3538952 | tf_op jit(solution)/shard_map/ppermute | solution.py:12
  293.4 111.3 %copy-start.22 = (s32[8,4]{0,1:T(4,128)S(1)}, s32[8,4]{0,1:T(4,128)}, u32[]{:S(2)}) copy-start(s32[8,4]{0,1:T(4,128)} %copy.114) | copy-start | bytes 388
  321.9 206.9 %collective-permute-start.4 = (bf16[1024,1152]{0,1:T(8,128)(2,1)}, bf16[1024,1152]{0,1:T(8,128)(2,1)}, u32[]{:S(2)}, u32[]{:S(2)}) collective-permute-start(bf16[1024,1152]{0,1:T(8,128)(2,1)} %collective-permute-done.3), channel_id=1, source_target_pairs={{0,4},{4,8},{8,12},{12,16},{16,20},{20,24},{24,28},{28,32},{32,36}... | collective-permute-start | bytes 7077896 | tf_op jit(solution)/shard_map/ppermute | solution.py:12
  413.7 113.3 %collective-permute-start.6 = (f32[1024,288]{0,1:T(8,128)}, f32[1024,288]{0,1:T(8,128)}, u32[]{:S(2)}, u32[]{:S(2)}) collective-permute-start(f32[1024,288]{0,1:T(8,128)} %bitcast_add_fusion.2), channel_id=1, source_target_pairs={{0,4},{4,8},{8,12},{12,16},{16,20},{20,24},{24,28},{28,32},{32,36}... | collective-permute-start | bytes 3538952 | tf_op jit(solution)/shard_map/ppermute | solution.py:12
  418.0 4.1 copy-start.31
  427.2 155.7 %all-gather.14.cloned.1.call-start = ((), (), s32[]{:S(2)}) async-start(), calls=%async_computation.6 | async-start | bytes 1310720 | tf_op jit(solution)/shard_map/all_gather | solution.py:69
  513.0 6.6 copy-start.19
  527.0 45.7 %collective-permute-start.7 = (f32[1024,288]{0,1:T(8,128)}, f32[1024,288]{0,1:T(8,128)}, u32[]{:S(2)}, u32[]{:S(2)}) collective-permute-start(f32[1024,288]{0,1:T(8,128)} %collective-permute-done.6), channel_id=1, source_target_pairs={{0,4},{4,8},{8,12},{12,16},{16,20},{20,24},{24,28},{28,32},{32,36}... | collective-permute-start | bytes 3538952 | tf_op jit(solution)/shard_map/ppermute | solution.py:12
  537.3 7.2 copy-start.18
  542.5 822.5 %all-reduce.10.cloned.1.call-start = ((), (), s32[]{:S(2)}) async-start(), calls=%async_computation.7 | async-start | bytes 5308416
  547.8 18.7 %copy-start.21 = (s32[8,4]{0,1:T(4,128)S(1)}, s32[8,4]{0,1:T(4,128)}, u32[]{:S(2)}) copy-start(s32[8,4]{0,1:T(4,128)} %copy.117) | copy-start | bytes 388
  572.6 3.0 copy-start.8
  572.6 3.0 copy-start.12
  572.6 3.0 copy-start.29
  575.5 51.7 %collective-permute-start.8 = (f32[1024,288]{0,1:T(8,128)}, f32[1024,288]{0,1:T(8,128)}, u32[]{:S(2)}, u32[]{:S(2)}) collective-permute-start(f32[1024,288]{0,1:T(8,128)} %bitcast_add_fusion.1), channel_id=1, source_target_pairs={{0,4},{4,8},{8,12},{12,16},{16,20},{20,24},{24,28},{28,32},{32,36}... | collective-permute-start | bytes 3538952 | tf_op jit(solution)/shard_map/ppermute | solution.py:12
  575.7 3.9 copy-start.17
  582.9 2.2 copy-start.20
  591.2 38.9 %copy-start.7 = (bf16[32,128,288]{1,2,0:T(8,128)(2,1)S(1)}, bf16[32,128,288]{1,2,0:T(8,128)(2,1)}, u32[]{:S(2)}) copy-start(bf16[32,128,288]{1,2,0:T(8,128)(2,1)} %gather_fusion.5) | copy-start | bytes 7077892
  591.2 38.9 %copy-start.13 = (bf16[8,4,128,128]{3,2,1,0:T(8,128)(2,1)S(1)}, bf16[8,4,128,128]{3,2,1,0:T(8,128)(2,1)}, u32[]{:S(2)}) copy-start(bf16[8,4,128,128]{3,2,1,0:T(8,128)(2,1)} %all-gather.12.cloned.1.call-done) | copy-start | bytes 3145732
  591.2 38.9 %copy-start.28 = (pred[8,4]{1,0:T(8,128)(4,1)S(1)}, pred[8,4]{1,0:T(8,128)(4,1)}, u32[]{:S(2)}) copy-start(pred[8,4]{1,0:T(8,128)(4,1)} %get-tuple-element.28) | copy-start | bytes 100
  629.9 29.6 %collective-permute-start.9 = (f32[1024,288]{0,1:T(8,128)}, f32[1024,288]{0,1:T(8,128)}, u32[]{:S(2)}, u32[]{:S(2)}) collective-permute-start(f32[1024,288]{0,1:T(8,128)} %bitcast_add_fusion), channel_id=1, source_target_pairs={{0,248},{4,252},{8,0},{12,4},{16,8},{20,12},{24,16},{28,20},{32,24... | collective-permute-start | bytes 3538952 | tf_op jit(solution)/shard_map/ppermute | solution.py:12
  634.0 3.3 copy-start.27
  637.3 3.0 copy-start.1
  637.3 3.0 copy-start.2
  637.3 3.1 copy-start.6
  637.3 3.5 copy-start.11
  640.7 18.8 %copy-start.4 = (bf16[1024,288]{0,1:T(8,128)(2,1)S(1)}, bf16[1024,288]{0,1:T(8,128)(2,1)}, u32[]{:S(2)}) copy-start(bf16[1024,288]{0,1:T(8,128)(2,1)} %copy-done.3) | copy-start | bytes 1769476
  670.0 3.9 copy-start.5
  670.0 3.9 copy-start.10
  677.3 0.7 copy-start.33
Sparse Core Ops, SparseCore 0:
  20.4 36.0 all-gather.5
  199.6 66.6 all-gather.7
  268.1 134.4 all-gather.9
  405.0 107.9 all-reduce.7
  514.7 49.5 all-gather.11
  566.0 16.3 all-gather.13
  677.5 687.4 all-reduce.9
where the time goes:
time: 1390 us; the launch traced here: 1380 us
  waiting for transfers between devices  1130 us (81%)
  local copies, waits for them, and re-layouts  94.1 us (7%)
  matrix products  79.9 us (6%)
  other arithmetic  29.9 us (2%)
  between operations  16.7 us (1%)
  starting transfers between devices  14.7 us (1%)
    unnamed x8, waiting for transfers between devices  686 us
    ppermute x10, waiting for transfers between devices, shifted(): return lax.ppermute(value, axis, pairs)  171 us
    all_gather x4, waiting for transfers between devices, shards(): pair_weight = lax.all_gather(weight_part, 'mp', axis=0, tiled=True)  96.9 us
    psum x1, waiting for transfers between devices, shards(): scores = lax.psum(partial_value, 'mp')  85.8 us
    all_to_all x1, waiting for transfers between devices, shards(): lax.all_to_all(image_unit, 'mp', split_axis=0, concat_axis=1, tiled=True)  51.7 us
    all_gather x1, waiting for transfers between devices, shards(): text_full = lax.all_gather(text_unit, 'mp', axis=1, tiled=True)  36.2 us
  transfers between devices with their start and end apart: 18, of which 11 were waited for; matrix products, arithmetic and copies ran while one was open for 13% of the time, Pallas kernels for 0%

commit v1 on v0

--- a/solution.py
+++ b/solution.py
@@ -38,7 +38,7 @@
     mine_tiles = image_mine.reshape(tiles_share, 128, image_mine.shape[1])
     text_full = lax.all_gather(text_unit, "mp", axis=1, tiled=True)
     partial_value = jnp.dot(image_unit, text_unit.T, preferred_element_type=jnp.float32)
-    scores = lax.psum(partial_value, "mp")
+    scores = jnp.sum(lax.all_gather(partial_value, "mp"), axis=0)
     diagonal_mask = jnp.eye(row_count, dtype=jnp.float32)
     weight = (
         temp_scale * (jax.nn.sigmoid(temp_scale * scores + shift_bias) - diagonal_mask)

time: 1390 us -> 1410 us (1.014)
    all_gather x0 -> x1, waiting for transfers between devices: none -> 110 us  [shards(): scores = jnp.sum(lax.all_gather(partial_value, 'mp'), axis=0)]
    all_gather x4, waiting for transfers between devices: 96.9 us -> 0.01 us  [shards(): pair_weight = lax.all_gather(weight_part, 'mp', axis=0, tiled=True)]
    psum x1 -> x0, waiting for transfers between devices: 85.8 us -> none  [shards(): scores = lax.psum(partial_value, 'mp')]
    ppermute x10, waiting for transfers between devices: 171 us -> 245 us  [shifted(): return lax.ppermute(value, axis, pairs)]
  transfers between devices with their start and end apart: 18 -> 18, of which waited for: 11 -> 12; matrix products, arithmetic and copies ran while one was open for 13% -> 14% of each run, Pallas kernels for 0% -> 0%
where the time goes in v1:
time: 1410 us; the launch traced here: 1400 us
  waiting for transfers between devices  1140 us (81%)
  local copies, waits for them, and re-layouts  95.4 us (7%)
  matrix products  80.6 us (6%)
  other arithmetic  39.9 us (3%)
  between operations  16.9 us (1%)
  blocking collectives  14.7 us (1%)
    unnamed x8, waiting for transfers between devices  697 us
    ppermute x10, waiting for transfers between devices, shifted(): return lax.ppermute(value, axis, pairs)  245 us
    all_gather x1, waiting for transfers between devices, shards(): scores = jnp.sum(lax.all_gather(partial_value, 'mp'), axis=0)  110 us
    all_to_all x1, waiting for transfers between devices, shards(): lax.all_to_all(image_unit, 'mp', split_axis=0, concat_axis=1, tiled=True)  51 us
    all_gather x1, waiting for transfers between devices, shards(): text_full = lax.all_gather(text_unit, 'mp', axis=1, tiled=True)  36.2 us
  transfers between devices with their start and end apart: 18, of which 12 were waited for; matrix products, arithmetic and copies ran while one was open for 14% of the time, Pallas kernels for 0%

profile of v1, /device:TPU:24, one launch (start us, length us, event | category | flops | bytes accessed | tf_op | source)
XLA Modules:
  0.0 1400.8 jit_solution(6495815879669699268)
XLA Ops:
  8.8 3.2 multiply_reduce_fusion.3
  13.0 6.3 all-reduce.4
  20.3 36.2 %all-gather.8.cloned.1.call-done = bf16[1024,1152]{0,1:T(8,128)(2,1)} async-done(((bf16[1024,288]{0,1:T(8,128)(2,1)}), bf16[1024,1152]{0,1:T(8,128)(2,1)}) %all-gather.8.cloned.1.call-update) | async-done | bytes 2359312 | tf_op jit(solution)/shard_map/all_gather | solution.py:39
  56.5 6.3 collective-permute-start
  62.8 51.6 %collective-permute-done = bf16[1024,1152]{0,1:T(8,128)(2,1)S(1)} collective-permute-done((bf16[1024,1152]{0,1:T(8,128)(2,1)}, bf16[1024,1152]{0,1:T(8,128)(2,1)S(1)}, u32[]{:S(2)}, u32[]{:S(2)}) %collective-permute-start) | collective-permute-done | bytes 2359328 | tf_op jit(solution)/shard_map/ppermute | solution.py:12
  116.5 58.8 %collective-permute-done.1 = bf16[1024,1152]{0,1:T(8,128)(2,1)} collective-permute-done((bf16[1024,1152]{0,1:T(8,128)(2,1)S(1)}, bf16[1024,1152]{0,1:T(8,128)(2,1)}, u32[]{:S(2)}, u32[]{:S(2)}) %collective-permute-start.1) | collective-permute-done | bytes 2359328 | tf_op jit(solution)/shard_map/ppermute | solution.py:12
  178.4 5.0 all-to-all-start
  189.1 51.0 %all-to-all-done = bf16[4,256,288]{1,2,0:T(8,128)(2,1)} async-done(((bf16[4,256,288]{1,2,0:T(8,128)(2,1)}), bf16[4,256,288]{1,2,0:T(8,128)(2,1)}, u32[]{:S(2)}, u32[]{:S(2)}) %all-to-all-start) | async-done | bytes 589856 | tf_op jit(solution)/shard_map/all_to_all | solution.py:37
  240.1 2.5 reshape.81
  242.6 2.9 copy.125
  245.5 4.4 copy.141
  249.9 4.1 gather_fusion
  254.0 3.3 fusion.160
  262.8 4.4 copy.144
  267.2 4.1 gather_fusion.2
  271.2 3.3 fusion.148
  274.6 1.8 copy.98
  276.5 25.5 %collective-permute-done.3 = bf16[1024,1152]{0,1:T(8,128)(2,1)} collective-permute-done((bf16[1024,1152]{0,1:T(8,128)(2,1)}, bf16[1024,1152]{0,1:T(8,128)(2,1)}, u32[]{:S(2)}, u32[]{:S(2)}) %collective-permute-start.3) | collective-permute-done | bytes 2359328 | tf_op jit(solution)/shard_map/ppermute | solution.py:12
  305.0 4.4 copy.147
  309.4 4.0 gather_fusion.4
  313.4 3.3 fusion.136
  316.7 1.8 copy.103
  322.6 37.8 %collective-permute-done.4 = bf16[1024,1152]{0,1:T(8,128)(2,1)} collective-permute-done((bf16[1024,1152]{0,1:T(8,128)(2,1)}, bf16[1024,1152]{0,1:T(8,128)(2,1)}, u32[]{:S(2)}, u32[]{:S(2)}) %collective-permute-start.4) | collective-permute-done | bytes 2359328 | tf_op jit(solution)/shard_map/ppermute | solution.py:12
  360.4 4.4 copy.150
  364.8 4.0 gather_fusion.6
  368.8 3.3 fusion.124
  372.1 1.8 copy.108
  374.0 4.5 fusion.197
  382.3 2.2 fusion.168
  384.5 6.1 fusion.6
  394.8 2.2 fusion.170
  397.0 6.1 fusion.4
  403.1 21.4 %collective-permute-done.5 = f32[1024,288]{0,1:T(8,128)} collective-permute-done((f32[1024,288]{0,1:T(8,128)}, f32[1024,288]{0,1:T(8,128)}, u32[]{:S(2)}, u32[]{:S(2)}) %collective-permute-start.5) | collective-permute-done | bytes 1179680 | tf_op jit(solution)/shard_map/ppermute | solution.py:12
  424.5 2.6 bitcast_add_fusion.2
  437.5 2.0 copy_bitcast_fusion.4
  439.5 3.5 gather_fusion.1
  443.0 3.8 fusion.32
  446.8 2.0 copy_bitcast_fusion.3
  448.8 3.3 gather_fusion.3
  452.1 6.3 collective-permute-done.6
  458.6 3.9 fusion.35
  462.5 2.0 copy_bitcast_fusion.2
  464.5 3.3 gather_fusion.5
  467.9 2.2 fusion.172
  470.0 6.1 fusion.2
  476.2 12.8 collective-permute-done.7
  489.0 2.7 bitcast_add_fusion.1
  492.0 1.9 fusion.38
  493.8 2.0 copy_bitcast_fusion.1
  495.8 3.3 gather_fusion.7
  499.2 2.4 fusion.174
  501.6 6.1 fusion
  507.7 30.8 %collective-permute-done.8 = f32[1024,288]{0,1:T(8,128)} collective-permute-done((f32[1024,288]{0,1:T(8,128)}, f32[1024,288]{0,1:T(8,128)}, u32[]{:S(2)}, u32[]{:S(2)}) %collective-permute-start.8) | collective-permute-done | bytes 1179680 | tf_op jit(solution)/shard_map/ppermute | solution.py:12
  538.6 2.6 bitcast_add_fusion
  541.5 1.9 fusion.41
  543.4 110.3 %all-gather.18.cloned.1.call-done = f32[4096,1024]{1,0:T(8,128)} async-done(((f32[1024,1024]{1,0:T(8,128)}), f32[4096,1024]{1,0:T(8,128)}) %all-gather.18.cloned.1.call-update) | async-done | bytes 16777232 | tf_op jit(solution)/shard_map/all_gather | solution.py:41
  653.6 10.3 reduce_sum.47
  664.0 3.5 multiply_convert_fusion
  667.8 3.4 multiply_reduce_fusion.1
  671.2 3.1 multiply_reduce_fusion
  674.2 8.4 all-reduce.3
  683.4 3.9 convolution_bitcast_fusion.1
  687.2 3.5 convolution_bitcast_fusion
  692.6 697.3 %all-reduce.7.cloned.1.call-done = (f32[1152,288]{0,1:T(8,128)}, f32[1152,288]{0,1:T(8,128)}) async-done(((f32[1152,288]{0,1:T(8,128)}, f32[1152,288]{0,1:T(8,128)}), (f32[1152,288]{0,1:T(8,128)}, f32[1152,288]{0,1:T(8,128)})) %all-reduce.7.cloned.1.call-update) | async-done | bytes 2654224
  (134 shorter events, 50.6 us)
Async XLA Ops:
  7.2 1.7 copy-start
  7.2 49.3 %all-gather.8.cloned.1.call-start = ((), (), s32[]{:S(2)}) async-start(), calls=%async_computation.1 | async-start | bytes 2949120 | tf_op jit(solution)/shard_map/all_gather | solution.py:39
  8.8 3.2 copy-start.9
  8.8 3.2 copy-start.29
  19.3 156.0 %copy-start.18 = (f32[1024]{0:T(1024)}, f32[1024]{0:T(1024)S(1)}, u32[]{:S(2)}) copy-start(f32[1024]{0:T(1024)S(1)} %get-tuple-element.17) | copy-start | bytes 12292
  19.3 159.1 %copy-start.17 = (f32[1024]{0:T(1024)}, f32[1024]{0:T(1024)S(1)}, u32[]{:S(2)}) copy-start(f32[1024]{0:T(1024)S(1)} %get-tuple-element.16) | copy-start | bytes 12292
  20.3 164.5 %copy-start.25 = (s32[8,16]{1,0:T(8,128)S(1)}, s32[8,16]{1,0:T(8,128)}, u32[]{:S(2)}) copy-start(s32[8,16]{1,0:T(8,128)} %param.15) | copy-start | bytes 1540
  56.5 57.9 %collective-permute-start = (bf16[1024,1152]{0,1:T(8,128)(2,1)}, bf16[1024,1152]{0,1:T(8,128)(2,1)S(1)}, u32[]{:S(2)}, u32[]{:S(2)}) collective-permute-start(bf16[1024,1152]{0,1:T(8,128)(2,1)} %all-gather.8.cloned.1.call-done), channel_id=1, source_target_pairs={{0,248},{4,252},{8,0},{12,4},{16,8},{20,12},{24,16},{28,20},{32,24... | collective-permute-start | bytes 7077896 | tf_op jit(solution)/shard_map/ppermute | solution.py:12
  114.4 1.5 copy-start.8
  115.9 59.4 %collective-permute-start.1 = (bf16[1024,1152]{0,1:T(8,128)(2,1)S(1)}, bf16[1024,1152]{0,1:T(8,128)(2,1)}, u32[]{:S(2)}, u32[]{:S(2)}) collective-permute-start(bf16[1024,1152]{0,1:T(8,128)(2,1)S(1)} %collective-permute-done), channel_id=1, source_target_pairs={{0,4},{4,8},{8,12},{12,16},{16,20},{20,24},{24,28},{28,32},{32,36}... | collective-permute-start | bytes 7077896 | tf_op jit(solution)/shard_map/ppermute | solution.py:12
  175.3 67.3 %collective-permute-start.2 = (bf16[1024,1152]{0,1:T(8,128)(2,1)}, bf16[1024,1152]{0,1:T(8,128)(2,1)}, u32[]{:S(2)}, u32[]{:S(2)}) collective-permute-start(bf16[1024,1152]{0,1:T(8,128)(2,1)} %collective-permute-done.1), channel_id=1, source_target_pairs={{0,4},{4,8},{8,12},{12,16},{16,20},{20,24},{24,28},{28,32},{32,36}... | collective-permute-start | bytes 7077896 | tf_op jit(solution)/shard_map/ppermute | solution.py:12
  176.7 0.8 copy-start.2
  178.4 61.7 %all-to-all-start = ((bf16[4,256,288]{1,2,0:T(8,128)(2,1)}), bf16[4,256,288]{1,2,0:T(8,128)(2,1)}, u32[]{:S(2)}, u32[]{:S(2)}) async-start(bf16[4,256,288]{1,2,0:T(8,128)(2,1)} %bitcast.194), calls=%async_computation | async-start | bytes 1179648 | tf_op jit(solution)/shard_map/all_to_all | solution.py:37
  183.4 198.8 %all-gather.10.cloned.1.call-start = ((), (), s32[]{:S(2)}) async-start(), calls=%async_computation.2 | async-start | bytes 1310720 | tf_op jit(solution)/shard_map/all_gather | solution.py:69
  185.5 0.6 copy-start.16
  242.6 59.4 %collective-permute-start.3 = (bf16[1024,1152]{0,1:T(8,128)(2,1)}, bf16[1024,1152]{0,1:T(8,128)(2,1)}, u32[]{:S(2)}, u32[]{:S(2)}) collective-permute-start(bf16[1024,1152]{0,1:T(8,128)(2,1)} %collective-permute-done.2), channel_id=1, source_target_pairs={{0,4},{4,8},{8,12},{12,16},{16,20},{20,24},{24,28},{28,32},{32,36}... | collective-permute-start | bytes 7077896 | tf_op jit(solution)/shard_map/ppermute | solution.py:12
  259.1 135.7 %all-gather.12.cloned.1.call-start = ((), (), s32[]{:S(2)}) async-start(), calls=%async_computation.3 | async-start | bytes 1310720 | tf_op jit(solution)/shard_map/all_gather | solution.py:69
  276.4 191.5 %all-gather.14.cloned.1.call-start = ((), (), s32[]{:S(2)}) async-start(), calls=%async_computation.4 | async-start | bytes 1310720 | tf_op jit(solution)/shard_map/all_gather | solution.py:69
  302.0 58.4 %collective-permute-start.4 = (bf16[1024,1152]{0,1:T(8,128)(2,1)}, bf16[1024,1152]{0,1:T(8,128)(2,1)}, u32[]{:S(2)}, u32[]{:S(2)}) collective-permute-start(bf16[1024,1152]{0,1:T(8,128)(2,1)} %collective-permute-done.3), channel_id=1, source_target_pairs={{0,4},{4,8},{8,12},{12,16},{16,20},{20,24},{24,28},{28,32},{32,36}... | collective-permute-start | bytes 7077896 | tf_op jit(solution)/shard_map/ppermute | solution.py:12
  318.5 180.7 %all-gather.16.cloned.1.call-start = ((), (), s32[]{:S(2)}) async-start(), calls=%async_computation.5 | async-start | bytes 1310720 | tf_op jit(solution)/shard_map/all_gather | solution.py:69
  373.9 279.7 %all-gather.18.cloned.1.call-start = ((), (), s32[]{:S(2)}) async-start(), calls=%async_computation.6 | async-start | bytes 20971520 | tf_op jit(solution)/shard_map/all_gather | solution.py:41
  378.6 1011.3 %all-reduce.7.cloned.1.call-start = ((), (), s32[]{:S(2)}) async-start(), calls=%async_computation.7 | async-start | bytes 5308416
  382.3 2.2 copy-start.23
  391.8 32.7 %collective-permute-start.5 = (f32[1024,288]{0,1:T(8,128)}, f32[1024,288]{0,1:T(8,128)}, u32[]{:S(2)}, u32[]{:S(2)}) collective-permute-start(f32[1024,288]{0,1:T(8,128)} %bitcast.160), channel_id=1, source_target_pairs={{0,4},{4,8},{8,12},{12,16},{16,20},{20,24},{24,28},{28,32},{32,36}... | collective-permute-start | bytes 3538952 | tf_op jit(solution)/shard_map/ppermute | solution.py:12
  394.8 2.2 copy-start.24
  403.1 24.0 %copy-start.26 = (s32[32]{0:T(128)S(1)}, s32[32]{0:T(128)}, u32[]{:S(2)}) copy-start(s32[32]{0:T(128)} %reshape.207) | copy-start | bytes 388
  427.1 31.3 %collective-permute-start.6 = (f32[1024,288]{0,1:T(8,128)}, f32[1024,288]{0,1:T(8,128)}, u32[]{:S(2)}, u32[]{:S(2)}) collective-permute-start(f32[1024,288]{0,1:T(8,128)} %bitcast_add_fusion.2), channel_id=1, source_target_pairs={{0,4},{4,8},{8,12},{12,16},{16,20},{20,24},{24,28},{28,32},{32,36}... | collective-permute-start | bytes 3538952 | tf_op jit(solution)/shard_map/ppermute | solution.py:12
  443.0 5.8 copy-start.20
  458.5 30.5 %collective-permute-start.7 = (f32[1024,288]{0,1:T(8,128)}, f32[1024,288]{0,1:T(8,128)}, u32[]{:S(2)}, u32[]{:S(2)}) collective-permute-start(f32[1024,288]{0,1:T(8,128)} %collective-permute-done.6), channel_id=1, source_target_pairs={{0,4},{4,8},{8,12},{12,16},{16,20},{20,24},{24,28},{28,32},{32,36}... | collective-permute-start | bytes 3538952 | tf_op jit(solution)/shard_map/ppermute | solution.py:12
  467.9 2.2 copy-start.22
  476.2 15.8 %copy-start.7 = (bf16[32,128,288]{1,2,0:T(8,128)(2,1)S(1)}, bf16[32,128,288]{1,2,0:T(8,128)(2,1)}, u32[]{:S(2)}) copy-start(bf16[32,128,288]{1,2,0:T(8,128)(2,1)} %gather_fusion.5) | copy-start | bytes 7077892
  476.2 15.8 %copy-start.14 = (bf16[8,4,128,128]{3,2,1,0:T(8,128)(2,1)S(1)}, bf16[8,4,128,128]{3,2,1,0:T(8,128)(2,1)}, u32[]{:S(2)}) copy-start(bf16[8,4,128,128]{3,2,1,0:T(8,128)(2,1)} %all-gather.14.cloned.1.call-done) | copy-start | bytes 3145732
  476.2 15.8 %copy-start.28 = (pred[8,4]{1,0:T(8,128)(4,1)S(1)}, pred[8,4]{1,0:T(8,128)(4,1)}, u32[]{:S(2)}) copy-start(pred[8,4]{1,0:T(8,128)(4,1)} %get-tuple-element.28) | copy-start | bytes 100
  491.7 46.9 %collective-permute-start.8 = (f32[1024,288]{0,1:T(8,128)}, f32[1024,288]{0,1:T(8,128)}, u32[]{:S(2)}, u32[]{:S(2)}) collective-permute-start(f32[1024,288]{0,1:T(8,128)} %bitcast_add_fusion.1), channel_id=1, source_target_pairs={{0,4},{4,8},{8,12},{12,16},{16,20},{20,24},{24,28},{28,32},{32,36}... | collective-permute-start | bytes 3538952 | tf_op jit(solution)/shard_map/ppermute | solution.py:12
  491.9 3.9 copy-start.19
  499.2 2.4 copy-start.21
  507.7 33.7 %copy-start.6 = (bf16[32,128,288]{1,2,0:T(8,128)(2,1)S(1)}, bf16[32,128,288]{1,2,0:T(8,128)(2,1)}, u32[]{:S(2)}) copy-start(bf16[32,128,288]{1,2,0:T(8,128)(2,1)} %gather_fusion.7) | copy-start | bytes 7077892
  507.7 33.7 %copy-start.15 = (bf16[8,4,128,128]{3,2,1,0:T(8,128)(2,1)S(1)}, bf16[8,4,128,128]{3,2,1,0:T(8,128)(2,1)}, u32[]{:S(2)}) copy-start(bf16[8,4,128,128]{3,2,1,0:T(8,128)(2,1)} %all-gather.16.cloned.1.call-done) | copy-start | bytes 3145732
  507.7 33.8 %copy-start.27 = (pred[8,4]{1,0:T(8,128)(4,1)S(1)}, pred[8,4]{1,0:T(8,128)(4,1)}, u32[]{:S(2)}) copy-start(pred[8,4]{1,0:T(8,128)(4,1)} %get-tuple-element.27) | copy-start | bytes 100
  541.2 129.9 %collective-permute-start.9 = (f32[1024,288]{0,1:T(8,128)}, f32[1024,288]{0,1:T(8,128)}, u32[]{:S(2)}, u32[]{:S(2)}) collective-permute-start(f32[1024,288]{0,1:T(8,128)} %bitcast_add_fusion), channel_id=1, source_target_pairs={{0,248},{4,252},{8,0},{12,4},{16,8},{20,12},{24,16},{28,20},{32,24... | collective-permute-start | bytes 3538952 | tf_op jit(solution)/shard_map/ppermute | solution.py:12
  664.0 3.5 copy-start.1
  664.0 3.5 copy-start.5
  664.0 3.5 copy-start.11
  664.0 3.5 copy-start.12
  664.0 3.8 copy-start.13
  667.8 3.4 copy-start.3
  683.4 3.9 copy-start.4
  683.4 3.9 copy-start.10
  690.7 0.7 copy-start.30
Sparse Core Ops, SparseCore 0:
  20.4 36.0 all-gather.7
  259.2 99.9 all-gather.9
  361.1 16.9 all-gather.11
  379.8 49.4 all-gather.13
  430.9 59.6 all-gather.15
  492.2 161.3 all-gather.17
  690.8 698.9 all-reduce.6
